TPU v7x, 128 devices: a whole 4x4x4 slice. The times are simulated.
128 devices in a mesh: dp: 8 (over y, core), tensor: 16 (over z, x).
Axes of the slice: x: 4, y: 4, z: 4, core: 2. Of those that a mesh axis runs over, the one named last changes fastest.
Arguments:
- features: bfloat16 [1024, 4096], P('dp'), may hold values from -6 to 6
- enc_in: bfloat16 [4096, 2048], P(None, 'tensor'), may hold values from -0.09375 to 0.09375
- enc_out: bfloat16 [2048, 8192], P('tensor'), may hold values from -0.125 to 0.125
- noise: bfloat16 [1024, 4096], P('dp', 'tensor'), may hold values from -6 to 6
- in_weight: bfloat16 [4096, 16384], P('dp', 'tensor'), may hold values from -0.09375 to 0.09375
- out_weight: bfloat16 [4096, 16384], P('dp', 'tensor'), may hold values from -0.046875 to 0.046875
- probes: bfloat16 [2, 1024, 4096], P(None, 'dp'), may hold values from -6 to 6
Outputs:
- flowed: float32 [1024, 4096], P('dp', 'tensor')
- logdet: float32 [1024], P('dp')
All inputs are finite; a program needn't handle non-finite values.
Results may differ from a plain program's by a relative error of at most 0.017.
Values may be sent and summed in bfloat16 or wider, within the bound.
No kernel may reach another device: no remote copies, remote signals or barrier semaphores. Data moves between devices by JAX's collectives and lax.ppermute only.
A program may use at most 128 MiB of HBM per device.

v0:
```python
import jax
import jax.numpy as jnp
from jax import lax
from jax.sharding import PartitionSpec as P

L = 4096
PROBES = 2
TERMS = 3


def collect(partial_value):
    return lax.psum(partial_value.astype(jnp.bfloat16), "tensor")


def series(start, w_in, w_out, slope):
    start32 = start.astype(jnp.float32)
    current = start
    running = jnp.zeros((start.shape[1],), jnp.float32)
    for term_idx in range(TERMS):
        pulled = jnp.einsum("pbl,lh->pbh", current, w_out, preferred_element_type=jnp.float32)
        scaled = (pulled * slope[None]).astype(jnp.bfloat16)
        partial_value = jnp.einsum("pbh,lh->pbl", scaled, w_in, preferred_element_type=jnp.float32)
        current = collect(partial_value)
        coeff = (-1.0) ** term_idx / (term_idx + 1)
        running = running + coeff * jnp.sum(start32 * current.astype(jnp.float32), axis=(0, 2))
    return running


def local(features, enc_in, enc_out, noise, in_weight, out_weight, probes):
    hidden = jax.nn.silu(jnp.dot(features, enc_in, preferred_element_type=jnp.float32)).astype(
        jnp.bfloat16
    )
    partial_stats = jnp.dot(hidden, enc_out, preferred_element_type=jnp.float32)
    batch_rows = partial_stats.shape[0]
    moments = lax.psum_scatter(
        partial_stats.reshape(batch_rows, 2, L), "tensor", scatter_dimension=2, tiled=True
    )
    u_slice = (moments[:, 0] + jax.nn.softplus(moments[:, 1]) * noise.astype(jnp.float32)).astype(
        jnp.bfloat16
    )
    u_full = lax.all_gather(u_slice, "tensor", axis=1, tiled=True)
    w_in, w_out = (
        lax.all_gather(in_weight, "dp", axis=0, tiled=True),
        lax.all_gather(out_weight, "dp", axis=0, tiled=True),
    )
    pre_act = jnp.dot(u_full, w_in, preferred_element_type=jnp.float32)
    tanh_val = jnp.tanh(pre_act)
    squash = tanh_val.astype(jnp.bfloat16)
    slope = 1.0 - tanh_val * tanh_val
    branch_part = jnp.einsum("bh,lh->bl", squash, w_out, preferred_element_type=jnp.float32)
    flowed = u_slice.astype(jnp.float32) + lax.psum_scatter(
        branch_part.astype(jnp.bfloat16), "tensor", scatter_dimension=1, tiled=True
    ).astype(jnp.float32)
    running = series(probes, w_in, w_out, slope)
    logdet = running / PROBES
    return (flowed, logdet)


def solution(mesh):
    in_specs = (
        P("dp", None),
        P(None, "tensor"),
        P("tensor", None),
        P("dp", "tensor"),
        P("dp", "tensor"),
        P("dp", "tensor"),
        P(None, "dp", None),
    )
    out_specs = (P("dp", "tensor"), P("dp"))
    return jax.shard_map(local, mesh=mesh, in_specs=in_specs, out_specs=out_specs, check_vma=False)
```

profile of v0, /device:TPU:0, one launch (start us, length us, event | category | flops | bytes accessed | tf_op | source)
XLA Modules:
  0.0 636.0 jit_solution(1916886400833628591)
XLA Ops:
  7.2 1.5 copy-done
  8.8 4.6 fusion.52
  13.4 4.6 copy.12
  18.0 0.0 all-gather.4.cloned.1.call-start
  18.0 81.1 %reduce-scatter.3.cloned.1.call-done = f32[128,2,256]{2,0,1:T(8,128)} async-done(((f32[128,2,4096]{2,0,1:T(8,128)}), f32[128,2,256]{2,0,1:T(8,128)}) %reduce-scatter.3.cloned.1.call-update) | async-done | bytes 262160 | tf_op jit(solution)/shard_map/reduce_scatter | solution.py:35
  99.1 1.7 fusion.51
  100.9 0.7 all-gather.6.cloned.1.call-update
  101.6 0.5 all-gather.8.cloned.1.call-update
  102.2 42.0 %all-gather.4.cloned.1.call-done = bf16[128,4096]{1,0:T(8,128)(2,1)} async-done(((bf16[128,256]{1,0:T(8,128)(2,1)}), bf16[128,4096]{1,0:T(8,128)(2,1)}) %all-gather.4.cloned.1.call-update) | async-done | bytes 1048592 | tf_op jit(solution)/shard_map/all_gather | solution.py:41
  144.2 50.7 %all-gather.6.cloned.1.call-done = bf16[4096,1024]{1,0:T(8,128)(2,1)} async-done(((bf16[512,1024]{1,0:T(8,128)(2,1)}), bf16[4096,1024]{1,0:T(8,128)(2,1)}) %all-gather.6.cloned.1.call-update) | async-done | bytes 8388624 | tf_op jit(solution)/shard_map/all_gather | solution.py:43
  194.9 5.0 multiply_subtract_fusion
  199.8 46.4 %all-gather.8.cloned.1.call-done = bf16[4096,1024]{1,0:T(8,128)(2,1)} async-done(((bf16[512,1024]{1,0:T(8,128)(2,1)}), bf16[4096,1024]{1,0:T(8,128)(2,1)}) %all-gather.8.cloned.1.call-update) | async-done | bytes 8388624 | tf_op jit(solution)/shard_map/all_gather | solution.py:44
  246.3 12.2 %fusion.12 = bf16[2,128,4096]{2,1,0:T(8,128)(2,1)} fusion(bf16[4096,1024]{1,0:T(8,128)(2,1)} %all-gather.6.cloned.1.call-done, bf16[2,128,4096]{2,1,0:T(8,128)(2,1)} %param.13, bf16[4096,1024]{1,0:T(8,128)(2,1)} %all-gather.8.cloned.1.call-done, f32[128,1024]{1,0:T(8,128)S(1)} %get-tuple-element.5), kind=kOutput, calls=%fused_computation.15 | convolution fusion | flops 4296540160 | bytes 21495808 | tf_op jit(solution)/shard_map/pbh,lh->pbl/dot_general | solution.py:22
  258.5 91.5 %all-reduce.4.cloned.1.call-done = bf16[2,128,4096]{2,1,0:T(8,128)(2,1)} async-done(((bf16[2,128,4096]{2,1,0:T(8,128)(2,1)}), bf16[2,128,4096]{2,1,0:T(8,128)(2,1)}) %all-reduce.4.cloned.1.call-update) | async-done | bytes 2097168 | tf_op jit(solution)/shard_map/psum | solution.py:12
  350.1 12.2 %fusion.15 = bf16[2,128,4096]{2,1,0:T(8,128)(2,1)} fusion(bf16[4096,1024]{1,0:T(8,128)(2,1)} %all-gather.6.cloned.1.call-done, bf16[2,128,4096]{2,1,0:T(8,128)(2,1)} %all-reduce.4.cloned.1.call-done, bf16[4096,1024]{1,0:T(8,128)(2,1)} %all-gather.8.cloned.1.call-done, f32[128,1024]{1,0:T(8,128)S(1)} %get-tuple-element.5), kind=kOutput, calls=%fused_computation.16 | convolution fusion | flops 4296540160 | bytes 21495808 | tf_op jit(solution)/shard_map/pbh,lh->pbl/dot_general | solution.py:22
  362.3 0.2 reduce-scatter.5.cloned.1.call-start
  362.5 7.3 %convolution_convert_fusion = bf16[128,4096]{1,0:T(8,128)(2,1)} fusion(bf16[4096,1024]{1,0:T(8,128)(2,1)} %all-gather.8.cloned.1.call-done, bf16[128,1024]{1,0:T(8,128)(2,1)S(1)} %get-tuple-element.6), kind=kOutput, calls=%fused_computation.18 | convolution fusion | flops 1074266112 | bytes 9699328 | tf_op jit(solution)/shard_map/bh,lh->bl/dot_general | solution.py:50
  369.8 83.3 %all-reduce.6.cloned.1.call-done = bf16[2,128,4096]{2,1,0:T(8,128)(2,1)} async-done(((bf16[2,128,4096]{2,1,0:T(8,128)(2,1)}), bf16[2,128,4096]{2,1,0:T(8,128)(2,1)}) %all-reduce.6.cloned.1.call-update) | async-done | bytes 2097168 | tf_op jit(solution)/shard_map/psum | solution.py:12
  453.1 12.2 %fusion.18 = bf16[2,128,4096]{2,1,0:T(8,128)(2,1)} fusion(bf16[4096,1024]{1,0:T(8,128)(2,1)} %all-gather.6.cloned.1.call-done, bf16[2,128,4096]{2,1,0:T(8,128)(2,1)} %all-reduce.6.cloned.1.call-done, bf16[4096,1024]{1,0:T(8,128)(2,1)} %all-gather.8.cloned.1.call-done, f32[128,1024]{1,0:T(8,128)S(1)} %get-tuple-element.5), kind=kOutput, calls=%fused_computation.17 | convolution fusion | flops 4296540160 | bytes 21495808 | tf_op jit(solution)/shard_map/pbh,lh->pbl/dot_general | solution.py:22
  465.4 64.4 %reduce-scatter.5.cloned.1.call-done = bf16[128,256]{1,0:T(8,128)(2,1)} async-done(((bf16[128,4096]{1,0:T(8,128)(2,1)}), bf16[128,256]{1,0:T(8,128)(2,1)}) %reduce-scatter.5.cloned.1.call-update) | async-done | bytes 65552 | tf_op jit(solution)/shard_map/reduce_scatter | solution.py:51
  529.8 1.5 convert_add_fusion
  531.3 92.4 %all-reduce.8.cloned.1.call-done = bf16[2,128,4096]{2,1,0:T(8,128)(2,1)} async-done(((bf16[2,128,4096]{2,1,0:T(8,128)(2,1)}), bf16[2,128,4096]{2,1,0:T(8,128)(2,1)}) %all-reduce.8.cloned.1.call-update) | async-done | bytes 2097168 | tf_op jit(solution)/shard_map/psum | solution.py:12
  623.7 5.0 fusion.22
  628.7 0.5 add_multiply_fusion
  (17 shorter events, 0.4 us)
Async XLA Ops:
  7.2 1.6 copy-start
  7.2 91.9 %reduce-scatter.3.cloned.1.call-start = ((), (), s32[]{:S(2)}) async-start(), calls=%async_computation.2 | async-start | bytes 4456448 | tf_op jit(solution)/shard_map/reduce_scatter | solution.py:35
  17.9 81.2 %copy-start.2 = (bf16[128,256]{1,0:T(8,128)(2,1)S(1)}, bf16[128,256]{1,0:T(8,128)(2,1)}, u32[]{:S(2)}) copy-start(bf16[128,256]{1,0:T(8,128)(2,1)} %param.10) | copy-start | bytes 196612
  18.0 126.2 %all-gather.4.cloned.1.call-start = ((), (), s32[]{:S(2)}) async-start(), calls=%async_computation.3 | async-start | bytes 1114112 | tf_op jit(solution)/shard_map/all_gather | solution.py:41
  100.8 94.0 %all-gather.6.cloned.1.call-start = ((), (), s32[]{:S(2)}) async-start(), calls=%async_computation.4 | async-start | bytes 9437184 | tf_op jit(solution)/shard_map/all_gather | solution.py:43
  101.5 144.7 %all-gather.8.cloned.1.call-start = ((), (), s32[]{:S(2)}) async-start(), calls=%async_computation.5 | async-start | bytes 9437184 | tf_op jit(solution)/shard_map/all_gather | solution.py:44
  102.1 247.9 %all-reduce.4.cloned.1.call-start = ((), (), s32[]{:S(2)}) async-start(), calls=%async_computation.7 | async-start | bytes 4194304 | tf_op jit(solution)/shard_map/psum | solution.py:12
  258.5 194.7 %all-reduce.6.cloned.1.call-start = ((), (), s32[]{:S(2)}) async-start(), calls=%async_computation.8 | async-start | bytes 4194304 | tf_op jit(solution)/shard_map/psum | solution.py:12
  362.3 167.5 %reduce-scatter.5.cloned.1.call-start = ((), (), s32[]{:S(2)}) async-start(), calls=%async_computation.6 | async-start | bytes 1114112 | tf_op jit(solution)/shard_map/reduce_scatter | solution.py:51
  369.8 160.0 %copy-start.1 = (bf16[128,256]{1,0:T(8,128)(2,1)S(1)}, bf16[128,256]{1,0:T(8,128)(2,1)}, u32[]{:S(2)}) copy-start(bf16[128,256]{1,0:T(8,128)(2,1)} %fusion.51) | copy-start | bytes 196612
  369.8 253.9 %all-reduce.8.cloned.1.call-start = ((), (), s32[]{:S(2)}) async-start(), calls=%async_computation.9 | async-start | bytes 4194304 | tf_op jit(solution)/shard_map/psum | solution.py:12
Sparse Core Ops, SparseCore 0:
  18.1 80.9 reduce-scatter.2
  101.8 42.3 all-gather.3
  145.9 48.9 all-gather.5
  196.4 49.8 all-gather.7
  258.6 91.4 all-reduce.3
  362.4 90.7 all-reduce.5
  456.3 73.3 reduce-scatter.4
  533.1 90.5 all-reduce.7
where the time goes:
time: 636 us
  waiting for transfers between devices  553 us (87%)
  matrix products  53.4 us (8%)
  between operations  14.2 us (2%)
  other arithmetic  8.67 us (1%)
    psum x3, waiting for transfers between devices, collect(): return lax.psum(partial_value.astype(jnp.bfloat16), 'tensor')  267 us
    reduce_scatter x1, waiting for transfers between devices, local(): lax.psum_scatter(partial_stats.reshape(batch_rows, 2, L), 'tensor', scatt...  81.1 us
    reduce_scatter x1, waiting for transfers between devices, local(): lax.psum_scatter(branch_part.astype(jnp.bfloat16), 'tensor', scatter_dime...  64.4 us
    all_gather x1, waiting for transfers between devices, local(): lax.all_gather(in_weight, 'dp', axis=0, tiled=True)  50.7 us
    all_gather x1, waiting for transfers between devices, local(): lax.all_gather(out_weight, 'dp', axis=0, tiled=True)  46.4 us
    all_gather x1, waiting for transfers between devices, local(): u_full = lax.all_gather(u_slice, 'tensor', axis=1, tiled=True)  42 us
    dot_general x3, matrix products, series(): jnp.einsum('pbh,lh->pbl', scaled, w_in, preferred_element_type=jnp.float32)  36.6 us
  transfers between devices with their start and end apart: 8, of which 8 were waited for; matrix products, arithmetic and copies ran while one was open for 4% of the time, Pallas kernels for 0%

commit v1 on v0

--- a/solution.py
+++ b/solution.py
@@ -12,6 +12,38 @@
     return lax.psum(partial_value.astype(jnp.bfloat16), "tensor")
 
 
+def gather_dp(block):
+    n = lax.axis_size("dp")
+    ny = n // 2
+
+    def perm(fn):
+        return [(d, fn(d // 2, d % 2)) for d in range(n)]
+
+    up = perm(lambda y, c: 2 * ((y + 1) % ny) + c)
+    down = perm(lambda y, c: 2 * ((y - 1) % ny) + c)
+    swap = perm(lambda y, c: 2 * y + 1 - c)
+    fwd = perm(lambda y, c: 2 * ((y + 1) % ny) if c == 0 else 2 * ((y - 1) % ny) + 1)
+
+    from_below = lax.ppermute(block, "dp", up)
+    from_above = lax.ppermute(block, "dp", down)
+    partner = lax.ppermute(block, "dp", swap)
+    d = lax.axis_index("dp")
+    y, c = d // 2, d % 2
+    relay = jnp.where(c == 0, from_below, from_above)
+    far = lax.ppermute(relay, "dp", fwd)
+    partner_near = lax.ppermute(jnp.stack([from_below, from_above]), "dp", swap)
+    partner_far = lax.ppermute(far, "dp", swap)
+    stacked = jnp.stack(
+        [block, partner, from_below, from_above, far, partner_near[0], partner_near[1], partner_far]
+    )
+    target = jnp.arange(n)
+    rel = (target // 2 - y) % ny
+    same_pos = jnp.array([0, 3, 4, 2], jnp.int32)[rel]
+    other_pos = jnp.array([1, 6, 7, 5], jnp.int32)[rel]
+    order = jnp.where(target % 2 == c, same_pos, other_pos)
+    return jnp.take(stacked, order, axis=0)
+
+
 def series(start, w_in, w_out, slope):
     start32 = start.astype(jnp.float32)
     current = start
@@ -20,29 +52,37 @@
         pulled = jnp.einsum("pbl,lh->pbh", current, w_out, preferred_element_type=jnp.float32)
         scaled = (pulled * slope[None]).astype(jnp.bfloat16)
         partial_value = jnp.einsum("pbh,lh->pbl", scaled, w_in, preferred_element_type=jnp.float32)
-        current = collect(partial_value)
         coeff = (-1.0) ** term_idx / (term_idx + 1)
-        running = running + coeff * jnp.sum(start32 * current.astype(jnp.float32), axis=(0, 2))
+        if term_idx == TERMS - 1:
+            local_dot = jnp.sum(start32 * partial_value, axis=(0, 2))
+            running = running + coeff * lax.psum(local_dot, "tensor")
+        else:
+            current = collect(partial_value)
+            running = running + coeff * jnp.sum(start32 * current.astype(jnp.float32), axis=(0, 2))
     return running
 
 
 def local(features, enc_in, enc_out, noise, in_weight, out_weight, probes):
+    rows_here = in_weight.shape[0]
+    both = gather_dp(jnp.stack([in_weight, out_weight], axis=0).reshape(2 * rows_here, -1))
+    both = both.reshape(-1, 2, rows_here, both.shape[-1])
+    w_in = both[:, 0].reshape(-1, both.shape[-1])
+    w_out = both[:, 1].reshape(-1, both.shape[-1])
     hidden = jax.nn.silu(jnp.dot(features, enc_in, preferred_element_type=jnp.float32)).astype(
         jnp.bfloat16
     )
     partial_stats = jnp.dot(hidden, enc_out, preferred_element_type=jnp.float32)
     batch_rows = partial_stats.shape[0]
     moments = lax.psum_scatter(
-        partial_stats.reshape(batch_rows, 2, L), "tensor", scatter_dimension=2, tiled=True
-    )
+        partial_stats.astype(jnp.bfloat16).reshape(batch_rows, 2, L),
+        "tensor",
+        scatter_dimension=2,
+        tiled=True,
+    ).astype(jnp.float32)
     u_slice = (moments[:, 0] + jax.nn.softplus(moments[:, 1]) * noise.astype(jnp.float32)).astype(
         jnp.bfloat16
     )
     u_full = lax.all_gather(u_slice, "tensor", axis=1, tiled=True)
-    w_in, w_out = (
-        lax.all_gather(in_weight, "dp", axis=0, tiled=True),
-        lax.all_gather(out_weight, "dp", axis=0, tiled=True),
-    )
     pre_act = jnp.dot(u_full, w_in, preferred_element_type=jnp.float32)
     tanh_val = jnp.tanh(pre_act)
     squash = tanh_val.astype(jnp.bfloat16)

time: 636 us -> 501 us (0.79)
  waiting for transfers between devices: 553 us -> 300 us
  local copies, waits for them, and re-layouts: 6.13 us -> 60.3 us
  blocking collectives: 0 us -> 38.1 us
  other arithmetic: 8.67 us -> 28.8 us
  starting transfers between devices: 0.5 us -> 6.98 us
    all_gather x2 -> x0, waiting for transfers between devices: 97.1 us -> none  [the longest x1 50.7 us: local(): lax.all_gather(in_weight, 'dp', axis=0, tiled=True)]
    psum x3 -> x2, waiting for transfers between devices: 267 us -> 177 us  [collect(): return lax.psum(partial_value.astype(jnp.bfloat16), 'tensor')]
    reduce_scatter x1, waiting for transfers between devices: 81.1 us -> 0.01 us  [local(): lax.psum_scatter(partial_stats.astype(jnp.bfloat16).reshape(batch_rows, 2...]
    ppermute x0 -> x6, waiting for transfers between devices: none -> 58.6 us  [the longest x1 38.6 us: gather_dp(): from_below = lax.ppermute(block, 'dp', up)]
    all_gather x1, waiting for transfers between devices: 42 us -> 0.01 us  [local(): u_full = lax.all_gather(u_slice, 'tensor', axis=1, tiled=True)]
    psum x0 -> x1, blocking collectives: none -> 38.1 us  [series(): running = running + coeff * lax.psum(local_dot, 'tensor')]
    gather x0 -> x5, local copies, waits for them, and re-layouts: none -> 29.2 us  [the longest x3 27.9 us: gather_dp(): return jnp.take(stacked, order, axis=0)]
    unnamed x6 -> x20, local copies, waits for them, and re-layouts: 1.55 us -> 20.3 us
  transfers between devices with their start and end apart: 8 -> 11, of which waited for: 8 -> 5; matrix products, arithmetic and copies ran while one was open for 4% -> 21% of each run, Pallas kernels for 0% -> 0%
where the time goes in v1:
time: 501 us; the launch traced here: 500 us
  waiting for transfers between devices  300 us (60%)
  local copies, waits for them, and re-layouts  60.3 us (12%)
  matrix products  51.9 us (10%)
  blocking collectives  38.1 us (8%)
  other arithmetic  28.8 us (6%)
  between operations  13.9 us (3%)
  starting transfers between devices  6.98 us (1%)
    psum x2, waiting for transfers between devices, collect(): return lax.psum(partial_value.astype(jnp.bfloat16), 'tensor')  177 us
    reduce_scatter x1, waiting for transfers between devices, local(): lax.psum_scatter(branch_part.astype(jnp.bfloat16), 'tensor', scatter_dime...  64.3 us
    ppermute x1, waiting for transfers between devices, gather_dp(): from_below = lax.ppermute(block, 'dp', up)  38.6 us
    psum x1, blocking collectives, series(): running = running + coeff * lax.psum(local_dot, 'tensor')  38.1 us
    dot_general x3, matrix products, series(): jnp.einsum('pbh,lh->pbl', scaled, w_in, preferred_element_type=jnp.float32)  35.5 us
    gather x3, local copies, waits for them, and re-layouts, gather_dp(): return jnp.take(stacked, order, axis=0)  27.9 us
    unnamed x20, local copies, waits for them, and re-layouts  20.3 us
    ppermute x1, waiting for transfers between devices, gather_dp(): far = lax.ppermute(relay, 'dp', fwd)  19.9 us
  transfers between devices with their start and end apart: 11, of which 5 were waited for; matrix products, arithmetic and copies ran while one was open for 21% of the time, Pallas kernels for 0%

profile of v1, /device:TPU:0, one launch (start us, length us, event | category | flops | bytes accessed | tf_op | source)
XLA Modules:
  0.0 500.3 jit_solution(5756758044395138447)
XLA Ops:
  7.2 3.2 pad_maximum_fusion.2
  13.7 4.0 convolution_convert_fusion
  17.7 3.1 copy.15
  20.9 38.6 %collective-permute-done.1 = bf16[1024,1024]{1,0:T(8,128)(2,1)} collective-permute-done((bf16[1024,1024]{1,0:T(8,128)(2,1)}, bf16[1024,1024]{1,0:T(8,128)(2,1)}, u32[]{:S(2)}, u32[]{:S(2)}) %collective-permute-start.1) | collective-permute-done | bytes 2097184 | tf_op jit(solution)/shard_map/ppermute | solution.py:27
  59.5 4.6 pad_maximum_fusion.1
  64.1 3.1 broadcast_select_fusion.1
  71.8 3.2 bitcast_dynamic-update-slice_fusion.3
  74.9 19.9 %collective-permute-done.3 = bf16[1024,1024]{1,0:T(8,128)(2,1)} collective-permute-done((bf16[1024,1024]{1,0:T(8,128)(2,1)}, bf16[1024,1024]{1,0:T(8,128)(2,1)}, u32[]{:S(2)}, u32[]{:S(2)}) %collective-permute-start.3) | collective-permute-done | bytes 2097184 | tf_op jit(solution)/shard_map/ppermute | solution.py:33
  109.2 4.7 constant_dynamic-update-slice_fusion
  115.3 11.7 %fusion.21 = (bf16[8,512,1024]{2,1,0:T(8,128)(2,1)}, bf16[8,512,1024]{2,1,0:T(8,128)(2,1)}) fusion(bf16[8,1024,1024]{2,1,0:T(8,128)(2,1)} %bitcast_dynamic-update-slice_fusion), kind=kLoop, calls=%fused_computation.73 | loop fusion | bytes 33554432 | tf_op jit(solution)/shard_map/jit(_take)/gather | solution.py:44
  127.0 8.1 %gather_fusion.3 = bf16[8,512,1024]{2,1,0:T(8,128)(2,1)} fusion(bf16[8,512,1024]{2,1,0:T(8,128)(2,1)} %get-tuple-element.7, s32[1024]{0:T(1024)S(1)} %pad_clamp_fusion), kind=kCustom, calls=%fused_computation.3 | custom fusion | bytes 16777248 | tf_op jit(solution)/shard_map/jit(_take)/gather | solution.py:44
  135.1 8.2 %gather_fusion.2 = bf16[8,512,1024]{2,1,0:T(8,128)(2,1)} fusion(bf16[8,512,1024]{2,1,0:T(8,128)(2,1)} %get-tuple-element.6, s32[1024]{0:T(1024)S(1)} %pad_clamp_fusion), kind=kCustom, calls=%fused_computation.2 | custom fusion | bytes 16777248 | tf_op jit(solution)/shard_map/jit(_take)/gather | solution.py:44
  143.3 8.0 %pad_maximum_fusion = bf16[8,1024,1024]{2,1,0:T(8,128)(2,1)S(1)} fusion(bf16[8,512,1024]{2,1,0:T(8,128)(2,1)} %gather_fusion.3, bf16[8,512,1024]{2,1,0:T(8,128)(2,1)} %gather_fusion.2), kind=kLoop, calls=%fused_computation.4 | loop fusion | flops 33554432 | bytes 33554432
  153.4 6.2 %fusion.20 = (bf16[8,1,512,1024]{3,2,1,0:T(8,128)(2,1)}, bf16[8,1,512,1024]{3,2,1,0:T(8,128)(2,1)}) fusion(bf16[8,2,512,1024]{3,2,1,0:T(8,128)(2,1)S(1)} %broadcast_select_fusion), kind=kLoop, calls=%fused_computation.72 | loop fusion | bytes 33554432 | tf_op jit(solution)/shard_map/slice | solution.py:69
  159.6 5.1 %multiply_subtract_fusion = (f32[128,1024]{1,0:T(8,128)S(1)}, bf16[128,1024]{1,0:T(8,128)(2,1)S(1)}) fusion(bf16[128,4096]{1,0:T(8,128)(2,1)} %all-gather.2.cloned.1.call-done, bf16[4096,1024]{1,0:T(8,128)(2,1)} %bitcast.72), kind=kOutput, calls=%fused_computation.35 | convolution fusion | flops 1074135040 | bytes 10223616 | tf_op jit(solution)/shard_map/dot_general | solution.py:86
  164.7 11.6 %convolution_convert_fusion.2 = bf16[2,128,4096]{2,1,0:T(8,128)(2,1)} fusion(bf16[4096,1024,1]{1,0,2:T(8,128)(2,1)} %bitcast.73, bf16[4096,1024,1]{1,0,2:T(8,128)(2,1)} %bitcast.76, bf16[2,128,4096]{2,1,0:T(8,128)(2,1)S(1)} %copy-done.4, f32[128,1024]{1,0:T(8,128)S(1)} %get-tuple-element.8), kind=kOutput, calls=%fused_computation.11 | convolution fusion | flops 4296540160 | bytes 21495808 | tf_op jit(solution)/shard_map/pbh,lh->pbl/dot_general | solution.py:54
  176.4 7.3 %convolution_convert_fusion.3 = bf16[128,4096]{1,0:T(8,128)(2,1)} fusion(bf16[4096,1024]{1,0:T(8,128)(2,1)} %bitcast.77, bf16[128,1024]{1,0:T(8,128)(2,1)S(1)} %get-tuple-element.9), kind=kOutput, calls=%fused_computation.12 | convolution fusion | flops 1074266112 | bytes 9699328 | tf_op jit(solution)/shard_map/bh,lh->bl/dot_general | solution.py:90
  184.0 85.1 %all-reduce.3.cloned.1.call-done = bf16[2,128,4096]{2,1,0:T(8,128)(2,1)} async-done(((bf16[2,128,4096]{2,1,0:T(8,128)(2,1)}), bf16[2,128,4096]{2,1,0:T(8,128)(2,1)}) %all-reduce.3.cloned.1.call-update) | async-done | bytes 2097168 | tf_op jit(solution)/shard_map/psum | solution.py:12
  269.1 12.2 %convolution_convert_fusion.1 = bf16[2,128,4096]{2,1,0:T(8,128)(2,1)} fusion(bf16[4096,1024,1]{1,0,2:T(8,128)(2,1)} %bitcast.74, bf16[2,128,4096]{2,1,0:T(8,128)(2,1)} %all-reduce.3.cloned.1.call-done, bf16[4096,1024,1]{1,0,2:T(8,128)(2,1)} %bitcast.78, f32[128,1024]{1,0:T(8,128)S(1)} %get-tuple-element.8), kind=kOutput, calls=%fused_computation.10 | convolution fusion | flops 4296540160 | bytes 21495808 | tf_op jit(solution)/shard_map/pbh,lh->pbl/dot_general | solution.py:54
  281.3 64.3 %reduce-scatter.5.cloned.1.call-done = bf16[128,256]{1,0:T(8,128)(2,1)} async-done(((bf16[128,4096]{1,0:T(8,128)(2,1)}), bf16[128,256]{1,0:T(8,128)(2,1)}) %reduce-scatter.5.cloned.1.call-update) | async-done | bytes 65552 | tf_op jit(solution)/shard_map/reduce_scatter | solution.py:91
  347.1 92.3 %all-reduce.5.cloned.1.call-done = bf16[2,128,4096]{2,1,0:T(8,128)(2,1)} async-done(((bf16[2,128,4096]{2,1,0:T(8,128)(2,1)}), bf16[2,128,4096]{2,1,0:T(8,128)(2,1)}) %all-reduce.5.cloned.1.call-update) | async-done | bytes 2097168 | tf_op jit(solution)/shard_map/psum | solution.py:12
  439.4 11.8 %fusion.2 = f32[128]{0:T(128)S(1)} fusion(bf16[4096,1024,1]{1,0,2:T(8,128)(2,1)} %bitcast.75, bf16[2,128,4096]{2,1,0:T(8,128)(2,1)} %param.15, bf16[2,128,4096]{2,1,0:T(8,128)(2,1)} %all-reduce.5.cloned.1.call-done, bf16[4096,1024,1]{1,0,2:T(8,128)(2,1)} %bitcast.79, f32[128,1024]{1,0:T(8,128)S(1)} %get-tuple-element.8), kind=kOutput, calls=%fused_computation.23 | convolution fusion | flops 4298637312 | bytes 21496320 | tf_op jit(solution)/shard_map/pbh,lh->pbl/dot_general | solution.py:54
  451.1 38.1 %psum.23 = f32[128]{0:T(128)S(1)} all-reduce(f32[128]{0:T(128)S(1)} %fusion.2), channel_id=1, replica_groups=mesh['dp'=8,'tensor'=16] {'tensor'}, use_global_device_ids=true, to_apply=%region_7.8 | all-reduce | flops 128 | bytes 1024 | tf_op jit(solution)/shard_map/psum | solution.py:58
  489.3 4.0 fusion.1
  (53 shorter events, 28.1 us)
Async XLA Ops:
  7.2 6.5 %copy-start = (bf16[128,8192]{1,0:T(8,128)(2,1)S(1)}, bf16[128,8192]{1,0:T(8,128)(2,1)}, u32[]{:S(2)}) copy-start(bf16[128,8192]{1,0:T(8,128)(2,1)} %param.11) | copy-start | bytes 6291460
  7.2 97.0 %reduce-scatter.3.cloned.1.call-start = ((), (), s32[]{:S(2)}) async-start(), calls=%async_computation.2 | async-start | bytes 2228224 | tf_op jit(solution)/shard_map/reduce_scatter | solution.py:76
  10.4 49.1 %collective-permute-start.1 = (bf16[1024,1024]{1,0:T(8,128)(2,1)}, bf16[1024,1024]{1,0:T(8,128)(2,1)}, u32[]{:S(2)}, u32[]{:S(2)}) collective-permute-start(bf16[1024,1024]{1,0:T(8,128)(2,1)} %bitcast.6), channel_id=1, source_target_pairs={{0,32},{16,48},{32,64},{48,80},{64,96},{80,112},{96,0},{112,16},{1... | collective-permute-start | bytes 6291464 | tf_op jit(solution)/shard_map/ppermute | solution.py:27
  12.1 47.4 %collective-permute-start.2 = (bf16[1024,1024]{1,0:T(8,128)(2,1)}, bf16[1024,1024]{1,0:T(8,128)(2,1)}, u32[]{:S(2)}, u32[]{:S(2)}) collective-permute-start(bf16[1024,1024]{1,0:T(8,128)(2,1)} %bitcast.6), channel_id=1, source_target_pairs={{0,96},{16,112},{32,0},{48,16},{64,32},{80,48},{96,64},{112,80},{1... | collective-permute-start | bytes 6291464 | tf_op jit(solution)/shard_map/ppermute | solution.py:28
  20.8 49.6 %copy-start.3 = (s32[4]{0:T(128)S(1)}, s32[4]{0:T(128)}, u32[]{:S(2)}) copy-start(s32[4]{0:T(128)} %constant.102.clone) | copy-start | bytes 52
  20.8 50.3 %copy-start.2 = (s32[4]{0:T(128)S(1)}, s32[4]{0:T(128)}, u32[]{:S(2)}) copy-start(s32[4]{0:T(128)} %constant.101.clone) | copy-start | bytes 52
  20.8 138.8 %all-gather.2.cloned.1.call-start = ((), (), s32[]{:S(2)}) async-start(), calls=%async_computation.3 | async-start | bytes 1114112 | tf_op jit(solution)/shard_map/all_gather | solution.py:85
  64.1 45.0 %collective-permute-start.4 = (bf16[2,1024,1024]{2,1,0:T(8,128)(2,1)}, bf16[2,1024,1024]{2,1,0:T(8,128)(2,1)}, u32[]{:S(2)}, u32[]{:S(2)}) collective-permute-start(bf16[2,1024,1024]{2,1,0:T(8,128)(2,1)} %pad_maximum_fusion.1), channel_id=1, source_target_pairs={{0,16},{16,0},{32,48},{48,32},{64,80},{80,64},{96,112},{112,96},{1... | collective-permute-start | bytes 12582920 | tf_op jit(solution)/shard_map/ppermute | solution.py:34
  67.3 27.6 %collective-permute-start.3 = (bf16[1024,1024]{1,0:T(8,128)(2,1)}, bf16[1024,1024]{1,0:T(8,128)(2,1)}, u32[]{:S(2)}, u32[]{:S(2)}) collective-permute-start(bf16[1024,1024]{1,0:T(8,128)(2,1)} %broadcast_select_fusion.1), channel_id=1, source_target_pairs={{0,32},{16,112},{32,64},{48,16},{64,96},{80,48},{96,0},{112,80},{1... | collective-permute-start | bytes 6291464 | tf_op jit(solution)/shard_map/ppermute | solution.py:33
  68.9 26.0 %collective-permute-start = (bf16[1024,1024]{1,0:T(8,128)(2,1)}, bf16[1024,1024]{1,0:T(8,128)(2,1)}, u32[]{:S(2)}, u32[]{:S(2)}) collective-permute-start(bf16[1024,1024]{1,0:T(8,128)(2,1)} %bitcast.6), channel_id=1, source_target_pairs={{0,16},{16,0},{32,48},{48,32},{64,80},{80,64},{96,112},{112,96},{1... | collective-permute-start | bytes 6291464 | tf_op jit(solution)/shard_map/ppermute | solution.py:29
  71.7 33.3 %copy-start.6 = (bf16[128,256]{1,0:T(8,128)(2,1)S(1)}, bf16[128,256]{1,0:T(8,128)(2,1)}, u32[]{:S(2)}) copy-start(bf16[128,256]{1,0:T(8,128)(2,1)} %param.12) | copy-start | bytes 196612
  94.8 19.0 %collective-permute-start.5 = (bf16[1024,1024]{1,0:T(8,128)(2,1)}, bf16[1024,1024]{1,0:T(8,128)(2,1)S(1)}, u32[]{:S(2)}, u32[]{:S(2)}) collective-permute-start(bf16[1024,1024]{1,0:T(8,128)(2,1)} %collective-permute-done.3), channel_id=1, source_target_pairs={{0,16},{16,0},{32,48},{48,32},{64,80},{80,64},{96,112},{112,96},{1... | collective-permute-start | bytes 6291464 | tf_op jit(solution)/shard_map/ppermute | solution.py:35
  105.8 163.2 %all-reduce.3.cloned.1.call-start = ((), (), s32[]{:S(2)}) async-start(), calls=%async_computation.5 | async-start | bytes 4194304 | tf_op jit(solution)/shard_map/psum | solution.py:12
  159.6 5.1 %copy-start.4 = (bf16[2,128,4096]{2,1,0:T(8,128)(2,1)S(1)}, bf16[2,128,4096]{2,1,0:T(8,128)(2,1)}, u32[]{:S(2)}) copy-start(bf16[2,128,4096]{2,1,0:T(8,128)(2,1)} %param.15) | copy-start | bytes 6291460
  176.4 169.2 %reduce-scatter.5.cloned.1.call-start = ((), (), s32[]{:S(2)}) async-start(), calls=%async_computation.4 | async-start | bytes 1114112 | tf_op jit(solution)/shard_map/reduce_scatter | solution.py:91
  183.7 161.9 %copy-start.5 = (bf16[128,256]{1,0:T(8,128)(2,1)S(1)}, bf16[128,256]{1,0:T(8,128)(2,1)}, u32[]{:S(2)}) copy-start(bf16[128,256]{1,0:T(8,128)(2,1)} %fusion.13) | copy-start | bytes 196612
  183.7 255.7 %all-reduce.5.cloned.1.call-start = ((), (), s32[]{:S(2)}) async-start(), calls=%async_computation.6 | async-start | bytes 4194304 | tf_op jit(solution)/shard_map/psum | solution.py:12
  439.4 54.4 %copy-start.1 = (bf16[128,8192]{1,0:T(8,128)(2,1)S(1)}, bf16[128,8192]{1,0:T(8,128)(2,1)}, u32[]{:S(2)}) copy-start(bf16[128,8192]{1,0:T(8,128)(2,1)} %param.11) | copy-start | bytes 6291460
Sparse Core Ops, SparseCore 0:
  20.9 76.7 reduce-scatter.2
  105.9 44.6 all-gather.1
  176.5 92.5 all-reduce.2
  272.1 73.4 reduce-scatter.4
  348.8 90.5 all-reduce.4
